TPU v7x, 512 devices: a whole 4x4x16 slice. The times are simulated.
512 devices in a mesh: seq: 128 (over z, x, core), fsdp: 4 (over y).
Axes of the slice: x: 4, y: 4, z: 16, core: 2. Of those that a mesh axis runs over, the one named last changes fastest.
Arguments:
- query_key: bfloat16 [131072, 3072], P(('seq', 'fsdp')), may hold values from -48 to 48
- values: bfloat16 [131072, 3072], P(('seq', 'fsdp')), may hold values from -6 to 6
- cluster_ids: int32 [24, 1024], replicated, may hold values from 0 to 127, as said below
Outputs:
- attended: bfloat16 [131072, 3072], P(('seq', 'fsdp'))
Inputs may be any that keep to these rules, and one draw needn't show every extreme that they name: `cluster_ids`: for every head and cluster at most 10 blocks name that cluster, and for every head some cluster is named by exactly 10 blocks. Among the (head, block) pairs of one group of 6 consecutive heads and one run of 8 blocks starting at a multiple of 8, no cluster is named more than 1 times, and some cluster exactly 1 times; the blocks of one such run name distinct clusters for each head.
All inputs are finite; a program needn't handle non-finite values.
Results may differ from a plain program's by a relative error of at most 0.0027.
Values may be sent and summed in bfloat16 or wider, within the bound.
No kernel may reach another device: no remote copies, remote signals or barrier semaphores. Data moves between devices by JAX's collectives and lax.ppermute only.
A program may use at most 64 MiB of HBM per device.

v0:
```python
import math
import jax
import jax.numpy as jnp
from jax import lax
from jax.sharding import PartitionSpec as P

BLK = 128
masked_score = -1e30


def by_index(source_table, row_index):
    padded = jnp.concatenate(
        [source_table, jnp.zeros((1,) + source_table.shape[1:], source_table.dtype)], axis=0
    )
    return padded[row_index]


def softmax_group(key_rows, positions, alive_rows, score_scale):
    half = BLK // 2
    blocks = key_rows.shape[0] // BLK

    def by_half(rows):
        shaped = rows.reshape((blocks, 2, half) + rows.shape[1:])
        return jnp.swapaxes(shaped, 0, 1).reshape(rows.shape)

    query_rows = by_half(key_rows)
    query_positions = by_half(positions)
    query_alive = by_half(alive_rows)
    scores = jnp.dot(query_rows, key_rows.T, preferred_element_type=jnp.float32) * score_scale
    allowed = alive_rows[None, :] & (positions[None, :] <= query_positions[:, None])
    scores = jnp.where(allowed, scores, masked_score)
    row_peak = jnp.max(scores, axis=1, keepdims=True)
    weights = jnp.where(allowed, jnp.exp(scores - row_peak), 0.0)
    row_total = jnp.where(query_alive[:, None], jnp.sum(weights, axis=1, keepdims=True), 1.0)
    weights = weights.astype(jnp.bfloat16).reshape(2, blocks * half, key_rows.shape[0])
    row_total = row_total.reshape(2, blocks * half, 1)
    return (weights[0], weights[1], row_total[0], row_total[1])


def shards(query_key, values, cluster_ids):
    seq_count = lax.axis_size("seq")
    group_count = lax.axis_size("fsdp")
    seq_index = lax.axis_index("seq")
    group_index = lax.axis_index("fsdp")
    heads_all = cluster_ids.shape[0]
    group_heads = heads_all // group_count
    head_dim = query_key.shape[1] // heads_all
    tok_rows = query_key.shape[0]
    shard_blocks = group_count * tok_rows // BLK
    all_blocks = cluster_ids.shape[1]
    item_count = group_heads * shard_blocks
    slot_count = max(1, item_count // seq_count)
    capacity = shard_blocks + min(shard_blocks // 4, seq_count - shard_blocks)
    group_rows = capacity * BLK
    send_rows = seq_count * slot_count
    score_scale = 1.0 / math.sqrt(head_dim)
    keys_local, values_local = (
        lax.all_to_all(query_key, "fsdp", split_axis=1, concat_axis=0, tiled=True),
        lax.all_to_all(values, "fsdp", split_axis=1, concat_axis=0, tiled=True),
    )

    def into_items(block_data):
        shaped = block_data.reshape(shard_blocks, BLK, group_heads, head_dim)
        return jnp.transpose(shaped, (2, 0, 1, 3)).reshape(item_count, BLK, head_dim)

    key_items = into_items(keys_local)
    value_items = into_items(values_local)
    group_ids = lax.dynamic_slice_in_dim(cluster_ids, group_index * group_heads, group_heads, 0)
    by_source = jnp.transpose(
        group_ids.reshape(group_heads, seq_count, shard_blocks), (1, 0, 2)
    ).reshape(seq_count, item_count)
    own_dest = lax.dynamic_index_in_dim(by_source, seq_index, 0, keepdims=False)
    item_ids = jnp.arange(item_count, dtype=jnp.int32)
    earlier = (own_dest[None, :] == own_dest[:, None]) & (item_ids[None, :] < item_ids[:, None])
    own_pos = own_dest * slot_count + jnp.sum(earlier.astype(jnp.int32), axis=1)
    row_ids = jnp.arange(send_rows, dtype=jnp.int32)
    slot_match = own_pos[None, :] == row_ids[:, None]
    send_pick = jnp.sum(jnp.where(slot_match, item_ids[None, :], 0), axis=1) + item_count * (
        1 - jnp.any(slot_match, axis=1).astype(jnp.int32)
    )
    received_mask = (by_source == seq_index).astype(jnp.int32)
    recv_pos = (
        jnp.arange(seq_count, dtype=jnp.int32)[:, None] * slot_count
        + jnp.cumsum(received_mask, axis=1)
        - received_mask
    )
    recv_by_head = jnp.transpose(
        recv_pos.reshape(seq_count, group_heads, shard_blocks), (1, 0, 2)
    ).reshape(group_heads * all_blocks)
    owned_mask = (group_ids == seq_index).astype(jnp.int32)
    ordinal = jnp.cumsum(owned_mask, axis=1) - owned_mask
    target = jnp.where(
        owned_mask > 0, jnp.arange(group_heads, dtype=jnp.int32)[:, None] * capacity + ordinal, -1
    ).reshape(group_heads * all_blocks)
    slot_ids = jnp.arange(group_heads * capacity, dtype=jnp.int32)
    matches = target[None, :] == slot_ids[:, None]
    present = jnp.any(matches, axis=1)
    source_row = jnp.sum(jnp.where(matches, recv_by_head[None, :], 0), axis=1) + send_rows * (
        1 - present.astype(jnp.int32)
    )
    block_ids = jnp.tile(jnp.arange(all_blocks, dtype=jnp.int32), group_heads)
    block_of = jnp.sum(jnp.where(matches, block_ids[None, :], 0), axis=1)
    arrived_k = lax.all_to_all(
        by_index(key_items, send_pick), "seq", split_axis=0, concat_axis=0, tiled=True
    )
    arrived_v = lax.all_to_all(
        by_index(value_items, send_pick), "seq", split_axis=0, concat_axis=0, tiled=True
    )
    key_grouped = by_index(arrived_k, source_row)
    value_grouped = by_index(arrived_v, source_row)
    positions = (block_of[:, None] * BLK + jnp.arange(BLK, dtype=jnp.int32)[None, :]).reshape(
        group_heads, group_rows
    )
    alive_rows = jnp.repeat(present, BLK).reshape(group_heads, group_rows)

    def one_head(operands):
        key_rows, where_at, alive_here = operands
        return softmax_group(key_rows, where_at, alive_here, score_scale)

    weights_0, weights_1, totals_0, totals_1 = lax.map(
        one_head, (key_grouped.reshape(group_heads, group_rows, head_dim), positions, alive_rows)
    )
    half = BLK // 2
    value_rows = value_grouped.reshape(group_heads, group_rows, head_dim)
    back_match = source_row[None, :] == row_ids[:, None]
    back_pick = jnp.sum(
        jnp.where(back_match, slot_ids[None, :], 0), axis=1
    ) + group_heads * capacity * (1 - jnp.any(back_match, axis=1).astype(jnp.int32))
    pieces = []
    for part in range(2):
        part_weights = (weights_0, weights_1)[part]
        weighted = jnp.einsum(
            "hqk,hkd->hqd", part_weights, value_rows, preferred_element_type=jnp.float32
        )
        part_total = (totals_0, totals_1)[part]
        outputs = (weighted / part_total).astype(jnp.bfloat16)
        outputs = outputs.reshape(group_heads * capacity, half, head_dim)
        returned = lax.all_to_all(
            by_index(outputs, back_pick), "seq", split_axis=0, concat_axis=0, tiled=True
        )
        own_output = by_index(returned, own_pos)
        token_major = jnp.transpose(
            own_output.reshape(group_heads, shard_blocks, half, head_dim), (1, 2, 0, 3)
        ).reshape(shard_blocks * half, group_heads * head_dim)
        pieces.append(lax.all_to_all(token_major, "fsdp", split_axis=0, concat_axis=1, tiled=True))
    own_blocks = tok_rows // BLK
    joined = jnp.stack(
        [piece.reshape(own_blocks, half, heads_all * head_dim) for piece in pieces], axis=1
    )
    return joined.reshape(tok_rows, heads_all * head_dim)


def solution(mesh):
    placed = (P(("seq", "fsdp"), None), P(("seq", "fsdp"), None), P())
    return jax.shard_map(
        shards, mesh=mesh, in_specs=placed, out_specs=P(("seq", "fsdp"), None), check_vma=False
    )
```

profile of v0, /device:TPU:32, one launch (start us, length us, event | category | flops | bytes accessed | tf_op | source)
XLA Modules:
  0.0 725.8 jit_solution(8790920589746454872)
XLA Ops:
  0.0 2.6 copy.104
  2.6 4.6 all-to-all-start
  7.2 1.4 convert_bitcast_fusion
  8.6 1.7 reduce-window.6
  14.1 1.3 fusion.11
  18.4 1.6 copy.110
  20.4 7.5 %all-to-all-done = bf16[256,4,768]{0,2,1:T(8,128)(2,1)S(1)} async-done(((bf16[256,4,768]{0,2,1:T(8,128)(2,1)}), bf16[256,4,768]{0,2,1:T(8,128)(2,1)S(1)}, u32[]{:S(2)}, u32[]{:S(2)}) %all-to-all-start) | async-done | bytes 1572896 | tf_op jit(solution)/shard_map/all_to_all | solution.py:58
  27.9 3.6 all-to-all-start.2
  32.5 2.4 copy.105
  34.8 2.5 reshape.280
  37.3 1.8 copy.106
  39.1 1.5 concatenate.24
  40.7 3.1 gather_fusion
  43.8 7.5 %all-to-all-done.2 = bf16[256,4,768]{0,2,1:T(8,128)(2,1)S(1)} async-done(((bf16[256,4,768]{0,2,1:T(8,128)(2,1)}), bf16[256,4,768]{0,2,1:T(8,128)(2,1)S(1)}, u32[]{:S(2)}, u32[]{:S(2)}) %all-to-all-start.2) | async-done | bytes 1572896 | tf_op jit(solution)/shard_map/all_to_all | solution.py:59
  51.3 19.5 %all-to-all-start.1 = ((bf16[128,128,128]{2,1,0:T(8,128)(2,1)}), bf16[128,128,128]{2,1,0:T(8,128)(2,1)}, u32[]{:S(2)}, u32[]{:S(2)}) async-start(bf16[128,128,128]{2,1,0:T(8,128)(2,1)} %gather_fusion), calls=%async_computation.1 | async-start | bytes 8388608 | tf_op jit(solution)/shard_map/all_to_all | solution.py:103
  70.8 1.2 copy.111
  72.7 1.8 copy.112
  74.5 1.5 concatenate.26
  76.1 3.1 gather_fusion.2
  79.2 179.2 %all-to-all-done.1 = bf16[128,128,128]{2,1,0:T(8,128)(2,1)} async-done(((bf16[128,128,128]{2,1,0:T(8,128)(2,1)}), bf16[128,128,128]{2,1,0:T(8,128)(2,1)}, u32[]{:S(2)}, u32[]{:S(2)}) %all-to-all-start.1) | async-done | bytes 4194336 | tf_op jit(solution)/shard_map/all_to_all | solution.py:103
  258.4 9.4 %all-to-all-start.3 = ((bf16[128,128,128]{2,1,0:T(8,128)(2,1)}), bf16[128,128,128]{2,1,0:T(8,128)(2,1)}, u32[]{:S(2)}, u32[]{:S(2)}) async-start(bf16[128,128,128]{2,1,0:T(8,128)(2,1)} %gather_fusion.2), calls=%async_computation.3 | async-start | bytes 8388608 | tf_op jit(solution)/shard_map/all_to_all | solution.py:106
  268.3 5.8 concatenate.25
  274.1 3.1 gather_fusion.1
  277.3 41.2 %while.16 = (s32[]{:T(128)}, bf16[6,640,1280]{1,2,0:T(8,128)(2,1)}, bf16[6,640,1280]{1,2,0:T(8,128)(2,1)}, f32[6,640,1]{1,0,2:T(8,128)S(1)}, f32[6,640,1]{1,0,2:...) while((s32[]{:T(128)}, bf16[6,640,1280]{1,2,0:T(8,128)(2,1)}, ...), condition=%wide.region_12.13_spmd, body=%wide.region_9.12_spmd.sunk | while | flops 437451520 | bytes 25025912 | solution.py:120
  277.6 1.8 fusion.29
  279.3 2.4 fusion.30
  281.8 2.0 fusion.31
  284.4 1.8 fusion.29
  286.2 2.4 fusion.30
  288.6 2.0 fusion.31
  291.3 1.8 fusion.29
  293.1 2.4 fusion.30
  295.5 2.0 fusion.31
  298.1 1.8 fusion.29
  299.9 2.4 fusion.30
  302.3 2.0 fusion.31
  305.0 1.8 fusion.29
  306.8 2.4 fusion.30
  309.2 2.0 fusion.31
  311.8 1.8 fusion.29
  313.6 2.4 fusion.30
  316.0 2.0 fusion.31
  318.5 137.1 %all-to-all-done.3 = bf16[128,128,128]{2,1,0:T(8,128)(2,1)} async-done(((bf16[128,128,128]{2,1,0:T(8,128)(2,1)}), bf16[128,128,128]{2,1,0:T(8,128)(2,1)}, u32[]{:S(2)}, u32[]{:S(2)}) %all-to-all-start.3) | async-done | bytes 4194336 | tf_op jit(solution)/shard_map/all_to_all | solution.py:106
  455.5 5.8 concatenate.27
  461.3 3.1 gather_fusion.3
  464.5 7.7 %divide_convert_fusion.1 = bf16[6,640,128]{2,1,0:T(8,128)(2,1)S(1)} fusion(f32[6,640]{1,0:T(8,128)S(1)} %bitcast.151, bf16[6,640,1280]{1,2,0:T(8,128)(2,1)} %get-tuple-element.50, bf16[6,1280,128]{2,1,0:T(8,128)(2,1)S(1)} %bitcast.140), kind=kOutput, calls=%fused_computation.26 | convolution fusion | flops 1259274240 | bytes 12794880 | tf_op jit(solution)/shard_map/hqk,hkd->hqd/dot_general | solution.py:132
  472.3 2.2 gather_fusion.4
  474.5 8.9 %all-to-all-start.4 = ((bf16[128,64,128]{2,1,0:T(8,128)(2,1)}), bf16[128,64,128]{2,1,0:T(8,128)(2,1)S(1)}, u32[]{:S(2)}, u32[]{:S(2)}) async-start(bf16[128,64,128]{2,1,0:T(8,128)(2,1)} %gather_fusion.4), calls=%async_computation.4 | async-start | bytes 4194304 | tf_op jit(solution)/shard_map/all_to_all | solution.py:138
  483.4 7.6 %divide_convert_fusion = bf16[6,640,128]{2,1,0:T(8,128)(2,1)S(1)} fusion(f32[6,640]{1,0:T(8,128)S(1)} %bitcast.152, bf16[6,640,1280]{1,2,0:T(8,128)(2,1)} %get-tuple-element.52, bf16[6,1280,128]{2,1,0:T(8,128)(2,1)} %bitcast.141), kind=kOutput, calls=%fused_computation.25 | convolution fusion | flops 1259274240 | bytes 12794880 | tf_op jit(solution)/shard_map/hqk,hkd->hqd/dot_general | solution.py:132
  491.0 2.1 gather_fusion.6
  493.2 88.5 %all-to-all-done.4 = bf16[128,64,128]{2,1,0:T(8,128)(2,1)S(1)} async-done(((bf16[128,64,128]{2,1,0:T(8,128)(2,1)}), bf16[128,64,128]{2,1,0:T(8,128)(2,1)S(1)}, u32[]{:S(2)}, u32[]{:S(2)}) %all-to-all-start.4) | async-done | bytes 2097184 | tf_op jit(solution)/shard_map/all_to_all | solution.py:138
  581.7 9.1 %all-to-all-start.6 = ((bf16[128,64,128]{2,1,0:T(8,128)(2,1)}), bf16[128,64,128]{2,1,0:T(8,128)(2,1)}, u32[]{:S(2)}, u32[]{:S(2)}) async-start(bf16[128,64,128]{2,1,0:T(8,128)(2,1)} %gather_fusion.6), calls=%async_computation.6 | async-start | bytes 4194304 | tf_op jit(solution)/shard_map/all_to_all | solution.py:138
  590.8 1.8 concatenate.29
  592.6 2.3 gather_fusion.5
  595.5 1.8 all_to_all.69
  597.3 91.5 %all-to-all-done.6 = bf16[128,64,128]{2,1,0:T(8,128)(2,1)} async-done(((bf16[128,64,128]{2,1,0:T(8,128)(2,1)}), bf16[128,64,128]{2,1,0:T(8,128)(2,1)}, u32[]{:S(2)}, u32[]{:S(2)}) %all-to-all-start.6) | async-done | bytes 2097184 | tf_op jit(solution)/shard_map/all_to_all | solution.py:138
  688.8 4.2 all-to-all-start.5
  693.0 2.0 concatenate.31
  696.3 1.8 all_to_all.73
  698.0 8.4 %all-to-all-done.5 = bf16[4,128,768]{2,1,0:T(8,128)(2,1)} async-done(((bf16[4,128,768]{2,1,0:T(8,128)(2,1)}), bf16[4,128,768]{2,1,0:T(8,128)(2,1)}, u32[]{:S(2)}, u32[]{:S(2)}) %all-to-all-start.5) | async-done | bytes 786464 | tf_op jit(solution)/shard_map/all_to_all | solution.py:145
  706.5 3.7 all-to-all-start.7
  710.2 1.7 copy.115
  712.5 10.5 %all-to-all-done.7 = bf16[4,128,768]{2,1,0:T(8,128)(2,1)S(1)} async-done(((bf16[4,128,768]{2,1,0:T(8,128)(2,1)}), bf16[4,128,768]{2,1,0:T(8,128)(2,1)S(1)}, u32[]{:S(2)}, u32[]{:S(2)}) %all-to-all-start.7) | async-done | bytes 786464 | tf_op jit(solution)/shard_map/all_to_all | solution.py:145
  724.3 1.2 copy.119
  (148 shorter events, 16.9 us)
Async XLA Ops:
  2.6 15.8 %copy-start.1 = (bf16[256,3072]{1,0:T(8,128)(2,1)S(1)}, bf16[256,3072]{1,0:T(8,128)(2,1)}, u32[]{:S(2)}) copy-start(bf16[256,3072]{1,0:T(8,128)(2,1)} %param.6) | copy-start | bytes 4718596
  2.6 25.3 %all-to-all-start = ((bf16[256,4,768]{0,2,1:T(8,128)(2,1)}), bf16[256,4,768]{0,2,1:T(8,128)(2,1)S(1)}, u32[]{:S(2)}, u32[]{:S(2)}) async-start(bf16[256,4,768]{0,2,1:T(8,128)(2,1)} %bitcast.13), calls=%async_computation | async-start | bytes 3145728 | tf_op jit(solution)/shard_map/all_to_all | solution.py:58
  17.1 2.9 copy-start.2
  17.1 3.1 copy-start.3
  20.0 11.5 %copy-start.4 = (s32[6144]{0:T(1024)S(1)}, s32[6144]{0:T(1024)}, u32[]{:S(2)}) copy-start(s32[6144]{0:T(1024)} %broadcast_in_dim.110) | copy-start | bytes 73732
  27.9 23.4 %all-to-all-start.2 = ((bf16[256,4,768]{0,2,1:T(8,128)(2,1)}), bf16[256,4,768]{0,2,1:T(8,128)(2,1)S(1)}, u32[]{:S(2)}, u32[]{:S(2)}) async-start(bf16[256,4,768]{0,2,1:T(8,128)(2,1)} %bitcast.132), calls=%async_computation.2 | async-start | bytes 3145728 | tf_op jit(solution)/shard_map/all_to_all | solution.py:59
  51.3 207.2 %all-to-all-start.1 = ((bf16[128,128,128]{2,1,0:T(8,128)(2,1)}), bf16[128,128,128]{2,1,0:T(8,128)(2,1)}, u32[]{:S(2)}, u32[]{:S(2)}) async-start(bf16[128,128,128]{2,1,0:T(8,128)(2,1)} %gather_fusion), calls=%async_computation.1 | async-start | bytes 8388608 | tf_op jit(solution)/shard_map/all_to_all | solution.py:103
  258.4 197.1 %all-to-all-start.3 = ((bf16[128,128,128]{2,1,0:T(8,128)(2,1)}), bf16[128,128,128]{2,1,0:T(8,128)(2,1)}, u32[]{:S(2)}, u32[]{:S(2)}) async-start(bf16[128,128,128]{2,1,0:T(8,128)(2,1)} %gather_fusion.2), calls=%async_computation.3 | async-start | bytes 8388608 | tf_op jit(solution)/shard_map/all_to_all | solution.py:106
  464.5 7.8 %copy-start = (bf16[60,128,128]{2,1,0:T(8,128)(2,1)}, bf16[60,128,128]{2,1,0:T(8,128)(2,1)S(1)}, u32[]{:S(2)}) copy-start(bf16[60,128,128]{2,1,0:T(8,128)(2,1)S(1)} %gather_fusion.3) | copy-start | bytes 5898244
  474.5 107.2 %all-to-all-start.4 = ((bf16[128,64,128]{2,1,0:T(8,128)(2,1)}), bf16[128,64,128]{2,1,0:T(8,128)(2,1)S(1)}, u32[]{:S(2)}, u32[]{:S(2)}) async-start(bf16[128,64,128]{2,1,0:T(8,128)(2,1)} %gather_fusion.4), calls=%async_computation.4 | async-start | bytes 4194304 | tf_op jit(solution)/shard_map/all_to_all | solution.py:138
  581.7 107.1 %all-to-all-start.6 = ((bf16[128,64,128]{2,1,0:T(8,128)(2,1)}), bf16[128,64,128]{2,1,0:T(8,128)(2,1)}, u32[]{:S(2)}, u32[]{:S(2)}) async-start(bf16[128,64,128]{2,1,0:T(8,128)(2,1)} %gather_fusion.6), calls=%async_computation.6 | async-start | bytes 4194304 | tf_op jit(solution)/shard_map/all_to_all | solution.py:138
  688.8 17.7 %all-to-all-start.5 = ((bf16[4,128,768]{2,1,0:T(8,128)(2,1)}), bf16[4,128,768]{2,1,0:T(8,128)(2,1)}, u32[]{:S(2)}, u32[]{:S(2)}) async-start(bf16[4,128,768]{2,1,0:T(8,128)(2,1)} %all_to_all.69), calls=%async_computation.5 | async-start | bytes 1572864 | tf_op jit(solution)/shard_map/all_to_all | solution.py:145
  706.5 16.5 %all-to-all-start.7 = ((bf16[4,128,768]{2,1,0:T(8,128)(2,1)}), bf16[4,128,768]{2,1,0:T(8,128)(2,1)S(1)}, u32[]{:S(2)}, u32[]{:S(2)}) async-start(bf16[4,128,768]{2,1,0:T(8,128)(2,1)} %all_to_all.73), calls=%async_computation.7 | async-start | bytes 1572864 | tf_op jit(solution)/shard_map/all_to_all | solution.py:145
where the time goes:
time: 735 us; the launch traced here: 726 us
  waiting for transfers between devices  530 us (72%)
  local copies, waits for them, and re-layouts  83.8 us (11%)
  starting transfers between devices  62.9 us (9%)
  matrix products  25.9 us (4%)
  other arithmetic  22 us (3%)
    all_to_all x2, waiting for transfers between devices, shards(): lax.all_to_all(by_index(outputs, back_pick), 'seq', split_axis=0, concat_...  180 us
    all_to_all x1, waiting for transfers between devices, shards(): lax.all_to_all(by_index(key_items, send_pick), 'seq', split_axis=0, conca...  179 us
    all_to_all x1, waiting for transfers between devices, shards(): lax.all_to_all(by_index(value_items, send_pick), 'seq', split_axis=0, con...  137 us
    gather x8, local copies, waits for them, and re-layouts, by_index(): return padded[row_index]  19.8 us
    all_to_all x1, starting transfers between devices, shards(): lax.all_to_all(by_index(key_items, send_pick), 'seq', split_axis=0, conca...  19.5 us
    all_to_all x2, waiting for transfers between devices, shards(): lax.all_to_all(token_major, 'fsdp', split_axis=0, concat_axis=1, tiled=True)  18.9 us
    concatenate x8, local copies, waits for them, and re-layouts, by_index(): jnp.concatenate([source_table, jnp.zeros((1,) + source_table.shape[1:], s...  18.7 us
    all_to_all x2, starting transfers between devices, shards(): lax.all_to_all(by_index(outputs, back_pick), 'seq', split_axis=0, concat_...  18 us
  transfers between devices with their start and end apart: 8, of which 8 were waited for; matrix products, arithmetic and copies ran while one was open for 14% of the time, Pallas kernels for 0%

commit v1 on v0

--- a/solution.py
+++ b/solution.py
@@ -6,6 +6,22 @@
 
 BLK = 128
 masked_score = -1e30
+
+
+def exchange_in_pairs(x, axis, split, join):
+    ways, here = (lax.axis_size(axis), lax.axis_index(axis))
+    width = x.shape[split] // ways
+    dims = list(x.shape)
+    dims[split] = width
+    height = dims[join]
+    dims[join] = height * ways
+    full = jnp.zeros(dims, x.dtype)
+    for mask in range(ways):
+        part = lax.dynamic_slice_in_dim(x, (here ^ mask) * width, width, axis=split)
+        if mask:
+            part = lax.ppermute(part, axis, [(d, d ^ mask) for d in range(ways)])
+        full = lax.dynamic_update_slice_in_dim(full, part, (here ^ mask) * height, axis=join)
+    return full
 
 
 def by_index(source_table, row_index):
@@ -142,7 +158,7 @@
         token_major = jnp.transpose(
             own_output.reshape(group_heads, shard_blocks, half, head_dim), (1, 2, 0, 3)
         ).reshape(shard_blocks * half, group_heads * head_dim)
-        pieces.append(lax.all_to_all(token_major, "fsdp", split_axis=0, concat_axis=1, tiled=True))
+        pieces.append(exchange_in_pairs(token_major, "fsdp", 0, 1))
     own_blocks = tok_rows // BLK
     joined = jnp.stack(
         [piece.reshape(own_blocks, half, heads_all * head_dim) for piece in pieces], axis=1

time: 735 us -> 726 us (0.988); the launches traced: 726 us -> 724 us
  waiting for transfers between devices: 530 us -> 519 us
  starting transfers between devices: 62.9 us -> 73.3 us
    all_to_all x2 -> x0, waiting for transfers between devices: 18.9 us -> none  [shards(): lax.all_to_all(token_major, 'fsdp', split_axis=0, concat_axis=1, tiled=True)]
    ppermute x0 -> x6, starting transfers between devices: none -> 18.7 us  [exchange_in_pairs(): part = lax.ppermute(part, axis, [(d, d ^ mask) for d in range(ways)])]
    ppermute x0 -> x6, waiting for transfers between devices: none -> 10.9 us  [exchange_in_pairs(): part = lax.ppermute(part, axis, [(d, d ^ mask) for d in range(ways)])]
    all_to_all x2 -> x0, starting transfers between devices: 7.9 us -> none  [shards(): lax.all_to_all(token_major, 'fsdp', split_axis=0, concat_axis=1, tiled=True)]
  transfers between devices with their start and end apart: 8 -> 12, of which waited for: 8 -> 9; matrix products, arithmetic and copies ran while one was open for 14% -> 15% of each run, Pallas kernels for 0% -> 0%
where the time goes in v1:
time: 726 us; the launch traced here: 724 us
  waiting for transfers between devices  519 us (71%)
  local copies, waits for them, and re-layouts  81.8 us (11%)
  starting transfers between devices  73.3 us (10%)
  matrix products  25.9 us (4%)
  other arithmetic  23.1 us (3%)
    all_to_all x1, waiting for transfers between devices, shards(): lax.all_to_all(by_index(key_items, send_pick), 'seq', split_axis=0, conca...  179 us
    all_to_all x2, waiting for transfers between devices, shards(): lax.all_to_all(by_index(outputs, back_pick), 'seq', split_axis=0, concat_...  177 us
    all_to_all x1, waiting for transfers between devices, shards(): lax.all_to_all(by_index(value_items, send_pick), 'seq', split_axis=0, con...  137 us
    gather x8, local copies, waits for them, and re-layouts, by_index(): return padded[row_index]  21.4 us
    concatenate x8, local copies, waits for them, and re-layouts, by_index(): jnp.concatenate([source_table, jnp.zeros((1,) + source_table.shape[1:], s...  20 us
    all_to_all x1, starting transfers between devices, shards(): lax.all_to_all(by_index(key_items, send_pick), 'seq', split_axis=0, conca...  19.5 us
    ppermute x6, starting transfers between devices, exchange_in_pairs(): part = lax.ppermute(part, axis, [(d, d ^ mask) for d in range(ways)])  18.7 us
    all_to_all x2, starting transfers between devices, shards(): lax.all_to_all(by_index(outputs, back_pick), 'seq', split_axis=0, concat_...  17.5 us
  transfers between devices with their start and end apart: 12, of which 9 were waited for; matrix products, arithmetic and copies ran while one was open for 15% of the time, Pallas kernels for 0%

profile of v1, /device:TPU:32, one launch (start us, length us, event | category | flops | bytes accessed | tf_op | source)
XLA Modules:
  0.0 724.3 jit_solution(8244968038627660337)
XLA Ops:
  0.0 2.6 copy.81
  2.6 4.6 all-to-all-start
  7.2 1.4 convert_bitcast_fusion
  8.6 1.7 reduce-window.6
  18.4 1.6 copy.87
  20.4 7.5 %all-to-all-done = bf16[256,4,768]{0,2,1:T(8,128)(2,1)S(1)} async-done(((bf16[256,4,768]{0,2,1:T(8,128)(2,1)}), bf16[256,4,768]{0,2,1:T(8,128)(2,1)S(1)}, u32[]{:S(2)}, u32[]{:S(2)}) %all-to-all-start) | async-done | bytes 1572896 | tf_op jit(solution)/shard_map/all_to_all | solution.py:74
  27.9 3.6 all-to-all-start.2
  32.5 2.4 copy.82
  34.8 2.5 reshape.274
  37.3 1.8 copy.83
  39.1 1.5 concatenate.24
  40.7 3.1 gather_fusion
  43.8 7.5 %all-to-all-done.2 = bf16[256,4,768]{0,2,1:T(8,128)(2,1)S(1)} async-done(((bf16[256,4,768]{0,2,1:T(8,128)(2,1)}), bf16[256,4,768]{0,2,1:T(8,128)(2,1)S(1)}, u32[]{:S(2)}, u32[]{:S(2)}) %all-to-all-start.2) | async-done | bytes 1572896 | tf_op jit(solution)/shard_map/all_to_all | solution.py:75
  51.3 19.5 %all-to-all-start.1 = ((bf16[128,128,128]{2,1,0:T(8,128)(2,1)}), bf16[128,128,128]{2,1,0:T(8,128)(2,1)}, u32[]{:S(2)}, u32[]{:S(2)}) async-start(bf16[128,128,128]{2,1,0:T(8,128)(2,1)} %gather_fusion), calls=%async_computation.1 | async-start | bytes 8388608 | tf_op jit(solution)/shard_map/all_to_all | solution.py:119
  72.7 1.8 copy.89
  74.5 1.5 concatenate.26
  76.1 3.1 gather_fusion.2
  79.2 179.2 %all-to-all-done.1 = bf16[128,128,128]{2,1,0:T(8,128)(2,1)} async-done(((bf16[128,128,128]{2,1,0:T(8,128)(2,1)}), bf16[128,128,128]{2,1,0:T(8,128)(2,1)}, u32[]{:S(2)}, u32[]{:S(2)}) %all-to-all-start.1) | async-done | bytes 4194336 | tf_op jit(solution)/shard_map/all_to_all | solution.py:119
  258.4 9.4 %all-to-all-start.3 = ((bf16[128,128,128]{2,1,0:T(8,128)(2,1)}), bf16[128,128,128]{2,1,0:T(8,128)(2,1)}, u32[]{:S(2)}, u32[]{:S(2)}) async-start(bf16[128,128,128]{2,1,0:T(8,128)(2,1)} %gather_fusion.2), calls=%async_computation.3 | async-start | bytes 8388608 | tf_op jit(solution)/shard_map/all_to_all | solution.py:122
  268.3 5.8 concatenate.25
  274.1 3.1 gather_fusion.1
  277.3 41.2 %while.16 = (s32[]{:T(128)}, bf16[6,640,1280]{1,2,0:T(8,128)(2,1)}, bf16[6,640,1280]{1,2,0:T(8,128)(2,1)}, f32[6,640,1]{1,0,2:T(8,128)S(1)}, f32[6,640,1]{1,0,2:...) while((s32[]{:T(128)}, bf16[6,640,1280]{1,2,0:T(8,128)(2,1)}, ...), condition=%wide.region_12.13_spmd, body=%wide.region_9.12_spmd.sunk | while | flops 437451520 | bytes 25025912 | solution.py:136
  277.6 1.8 fusion.29
  279.3 2.4 fusion.30
  281.8 2.0 fusion.31
  284.4 1.8 fusion.29
  286.2 2.4 fusion.30
  288.6 2.0 fusion.31
  291.3 1.8 fusion.29
  293.1 2.4 fusion.30
  295.5 2.0 fusion.31
  298.1 1.8 fusion.29
  299.9 2.4 fusion.30
  302.3 2.0 fusion.31
  305.0 1.8 fusion.29
  306.8 2.4 fusion.30
  309.2 2.0 fusion.31
  311.8 1.8 fusion.29
  313.6 2.4 fusion.30
  316.0 2.0 fusion.31
  318.5 137.1 %all-to-all-done.3 = bf16[128,128,128]{2,1,0:T(8,128)(2,1)} async-done(((bf16[128,128,128]{2,1,0:T(8,128)(2,1)}), bf16[128,128,128]{2,1,0:T(8,128)(2,1)}, u32[]{:S(2)}, u32[]{:S(2)}) %all-to-all-start.3) | async-done | bytes 4194336 | tf_op jit(solution)/shard_map/all_to_all | solution.py:122
  455.5 5.8 concatenate.27
  461.3 3.1 gather_fusion.3
  464.5 7.7 %divide_convert_fusion.1 = bf16[6,640,128]{2,1,0:T(8,128)(2,1)S(1)} fusion(f32[6,640]{1,0:T(8,128)S(1)} %bitcast.168, bf16[6,640,1280]{1,2,0:T(8,128)(2,1)} %get-tuple-element.50, bf16[6,1280,128]{2,1,0:T(8,128)(2,1)S(1)} %bitcast.157), kind=kOutput, calls=%fused_computation.26 | convolution fusion | flops 1259274240 | bytes 12794880 | tf_op jit(solution)/shard_map/hqk,hkd->hqd/dot_general | solution.py:148
  472.3 2.2 gather_fusion.4
  474.5 8.9 %all-to-all-start.4 = ((bf16[128,64,128]{2,1,0:T(8,128)(2,1)}), bf16[128,64,128]{2,1,0:T(8,128)(2,1)S(1)}, u32[]{:S(2)}, u32[]{:S(2)}) async-start(bf16[128,64,128]{2,1,0:T(8,128)(2,1)} %gather_fusion.4), calls=%async_computation.4 | async-start | bytes 4194304 | tf_op jit(solution)/shard_map/all_to_all | solution.py:154
  483.4 7.6 %divide_convert_fusion = bf16[6,640,128]{2,1,0:T(8,128)(2,1)S(1)} fusion(f32[6,640]{1,0:T(8,128)S(1)} %bitcast.169, bf16[6,640,1280]{1,2,0:T(8,128)(2,1)} %get-tuple-element.52, bf16[6,1280,128]{2,1,0:T(8,128)(2,1)} %bitcast.158), kind=kOutput, calls=%fused_computation.25 | convolution fusion | flops 1259274240 | bytes 12794880 | tf_op jit(solution)/shard_map/hqk,hkd->hqd/dot_general | solution.py:148
  491.1 2.1 gather_fusion.6
  493.2 88.5 %all-to-all-done.4 = bf16[128,64,128]{2,1,0:T(8,128)(2,1)S(1)} async-done(((bf16[128,64,128]{2,1,0:T(8,128)(2,1)}), bf16[128,64,128]{2,1,0:T(8,128)(2,1)S(1)}, u32[]{:S(2)}, u32[]{:S(2)}) %all-to-all-start.4) | async-done | bytes 2097184 | tf_op jit(solution)/shard_map/all_to_all | solution.py:154
  583.1 8.6 %all-to-all-start.5 = ((bf16[128,64,128]{2,1,0:T(8,128)(2,1)}), bf16[128,64,128]{2,1,0:T(8,128)(2,1)S(1)}, u32[]{:S(2)}, u32[]{:S(2)}) async-start(bf16[128,64,128]{2,1,0:T(8,128)(2,1)} %gather_fusion.6), calls=%async_computation.5 | async-start | bytes 4194304 | tf_op jit(solution)/shard_map/all_to_all | solution.py:154
  591.7 3.4 concatenate.29
  595.1 2.3 gather_fusion.5
  598.9 2.5 collective-permute-start
  601.4 88.6 %all-to-all-done.5 = bf16[128,64,128]{2,1,0:T(8,128)(2,1)S(1)} async-done(((bf16[128,64,128]{2,1,0:T(8,128)(2,1)}), bf16[128,64,128]{2,1,0:T(8,128)(2,1)S(1)}, u32[]{:S(2)}, u32[]{:S(2)}) %all-to-all-start.5) | async-done | bytes 2097184 | tf_op jit(solution)/shard_map/all_to_all | solution.py:154
  690.0 1.8 concatenate.31
  691.8 2.3 gather_fusion.7
  695.7 2.5 collective-permute-start.3
  698.2 4.0 collective-permute-start.1
  702.2 4.0 collective-permute-start.2
  706.1 1.9 collective-permute-start.4
  708.1 3.9 collective-permute-start.5
  712.1 4.9 collective-permute-done.4
  717.1 1.8 collective-permute-done.2
  718.8 4.2 collective-permute-done.5
  (163 shorter events, 21.5 us)
Async XLA Ops:
  2.6 15.8 %copy-start.2 = (bf16[256,3072]{1,0:T(8,128)(2,1)S(1)}, bf16[256,3072]{1,0:T(8,128)(2,1)}, u32[]{:S(2)}) copy-start(bf16[256,3072]{1,0:T(8,128)(2,1)} %param.6) | copy-start | bytes 4718596
  2.6 25.3 %all-to-all-start = ((bf16[256,4,768]{0,2,1:T(8,128)(2,1)}), bf16[256,4,768]{0,2,1:T(8,128)(2,1)S(1)}, u32[]{:S(2)}, u32[]{:S(2)}) async-start(bf16[256,4,768]{0,2,1:T(8,128)(2,1)} %bitcast.13), calls=%async_computation | async-start | bytes 3145728 | tf_op jit(solution)/shard_map/all_to_all | solution.py:74
  17.1 2.9 copy-start.3
  17.1 3.1 copy-start.4
  20.0 11.5 %copy-start.5 = (s32[6144]{0:T(1024)S(1)}, s32[6144]{0:T(1024)}, u32[]{:S(2)}) copy-start(s32[6144]{0:T(1024)} %broadcast_in_dim.110) | copy-start | bytes 73732
  27.9 23.4 %all-to-all-start.2 = ((bf16[256,4,768]{0,2,1:T(8,128)(2,1)}), bf16[256,4,768]{0,2,1:T(8,128)(2,1)S(1)}, u32[]{:S(2)}, u32[]{:S(2)}) async-start(bf16[256,4,768]{0,2,1:T(8,128)(2,1)} %bitcast.144), calls=%async_computation.2 | async-start | bytes 3145728 | tf_op jit(solution)/shard_map/all_to_all | solution.py:75
  51.3 207.2 %all-to-all-start.1 = ((bf16[128,128,128]{2,1,0:T(8,128)(2,1)}), bf16[128,128,128]{2,1,0:T(8,128)(2,1)}, u32[]{:S(2)}, u32[]{:S(2)}) async-start(bf16[128,128,128]{2,1,0:T(8,128)(2,1)} %gather_fusion), calls=%async_computation.1 | async-start | bytes 8388608 | tf_op jit(solution)/shard_map/all_to_all | solution.py:119
  258.4 197.1 %all-to-all-start.3 = ((bf16[128,128,128]{2,1,0:T(8,128)(2,1)}), bf16[128,128,128]{2,1,0:T(8,128)(2,1)}, u32[]{:S(2)}, u32[]{:S(2)}) async-start(bf16[128,128,128]{2,1,0:T(8,128)(2,1)} %gather_fusion.2), calls=%async_computation.3 | async-start | bytes 8388608 | tf_op jit(solution)/shard_map/all_to_all | solution.py:122
  464.5 7.8 %copy-start.1 = (bf16[60,128,128]{2,1,0:T(8,128)(2,1)}, bf16[60,128,128]{2,1,0:T(8,128)(2,1)S(1)}, u32[]{:S(2)}) copy-start(bf16[60,128,128]{2,1,0:T(8,128)(2,1)S(1)} %gather_fusion.3) | copy-start | bytes 5898244
  474.5 107.2 %all-to-all-start.4 = ((bf16[128,64,128]{2,1,0:T(8,128)(2,1)}), bf16[128,64,128]{2,1,0:T(8,128)(2,1)S(1)}, u32[]{:S(2)}, u32[]{:S(2)}) async-start(bf16[128,64,128]{2,1,0:T(8,128)(2,1)} %gather_fusion.4), calls=%async_computation.4 | async-start | bytes 4194304 | tf_op jit(solution)/shard_map/all_to_all | solution.py:154
  581.7 1.3 copy-start
  583.1 107.0 %all-to-all-start.5 = ((bf16[128,64,128]{2,1,0:T(8,128)(2,1)}), bf16[128,64,128]{2,1,0:T(8,128)(2,1)S(1)}, u32[]{:S(2)}, u32[]{:S(2)}) async-start(bf16[128,64,128]{2,1,0:T(8,128)(2,1)} %gather_fusion.6), calls=%async_computation.5 | async-start | bytes 4194304 | tf_op jit(solution)/shard_map/all_to_all | solution.py:154
  598.9 109.1 %collective-permute-start = (bf16[128,768]{1,0:T(8,128)(2,1)}, bf16[128,768]{1,0:T(8,128)(2,1)S(1)}, u32[]{:S(2)}, u32[]{:S(2)}) collective-permute-start(bf16[128,768]{1,0:T(8,128)(2,1)} %get-tuple-element.87), channel_id=1, source_target_pairs={{0,1},{1,0},{2,3},{3,2},{4,5},{5,4},{6,7},{7,6},{8,9},{9,8},{10,11... | collective-permute-start | bytes 589832 | tf_op jit(solution)/shard_map/ppermute | solution.py:22
  695.7 16.4 %collective-permute-start.3 = (bf16[128,768]{1,0:T(8,128)(2,1)}, bf16[128,768]{1,0:T(8,128)(2,1)S(1)}, u32[]{:S(2)}, u32[]{:S(2)}) collective-permute-start(bf16[128,768]{1,0:T(8,128)(2,1)} %get-tuple-element.91), channel_id=1, source_target_pairs={{0,1},{1,0},{2,3},{3,2},{4,5},{5,4},{6,7},{7,6},{8,9},{9,8},{10,11... | collective-permute-start | bytes 589832 | tf_op jit(solution)/shard_map/ppermute | solution.py:22
  698.2 13.9 %collective-permute-start.1 = (bf16[128,768]{1,0:T(8,128)(2,1)S(1)}, bf16[128,768]{1,0:T(8,128)(2,1)S(1)}, u32[]{:S(2)}, u32[]{:S(2)}) collective-permute-start(bf16[128,768]{1,0:T(8,128)(2,1)S(1)} %get-tuple-element.86), channel_id=1, source_target_pairs={{0,2},{1,3},{2,0},{3,1},{4,6},{5,7},{6,4},{7,5},{8,10},{9,11},{10,... | collective-permute-start | bytes 589832 | tf_op jit(solution)/shard_map/ppermute | solution.py:22
  702.2 16.7 %collective-permute-start.2 = (bf16[128,768]{1,0:T(8,128)(2,1)S(1)}, bf16[128,768]{1,0:T(8,128)(2,1)S(1)}, u32[]{:S(2)}, u32[]{:S(2)}) collective-permute-start(bf16[128,768]{1,0:T(8,128)(2,1)S(1)} %get-tuple-element.85), channel_id=1, source_target_pairs={{0,3},{1,2},{2,1},{3,0},{4,7},{5,6},{6,5},{7,4},{8,11},{9,10},{10,... | collective-permute-start | bytes 589832 | tf_op jit(solution)/shard_map/ppermute | solution.py:22
  706.1 10.9 %collective-permute-start.4 = (bf16[128,768]{1,0:T(8,128)(2,1)}, bf16[128,768]{1,0:T(8,128)(2,1)S(1)}, u32[]{:S(2)}, u32[]{:S(2)}) collective-permute-start(bf16[128,768]{1,0:T(8,128)(2,1)} %get-tuple-element.90), channel_id=1, source_target_pairs={{0,2},{1,3},{2,0},{3,1},{4,6},{5,7},{6,4},{7,5},{8,10},{9,11},{10,... | collective-permute-start | bytes 589832 | tf_op jit(solution)/shard_map/ppermute | solution.py:22
  708.1 14.9 %collective-permute-start.5 = (bf16[128,768]{1,0:T(8,128)(2,1)S(1)}, bf16[128,768]{1,0:T(8,128)(2,1)S(1)}, u32[]{:S(2)}, u32[]{:S(2)}) collective-permute-start(bf16[128,768]{1,0:T(8,128)(2,1)S(1)} %get-tuple-element.89), channel_id=1, source_target_pairs={{0,3},{1,2},{2,1},{3,0},{4,7},{5,6},{6,5},{7,4},{8,11},{9,10},{10,... | collective-permute-start | bytes 589832 | tf_op jit(solution)/shard_map/ppermute | solution.py:22
